TPU v7x, 512 devices: a whole 4x4x16 slice. The times are simulated.
512 devices in a mesh: chan: 32 (over z, x_hi), seg: 16 (over y, x_lo, core).
Axes of the slice: x: 4 (x_hi: 2, x_lo: 2; x = x_hi * 2 + x_lo), y: 4, z: 16, core: 2. Of those that a mesh axis runs over, the one named last changes fastest.
Arguments:
- traces: bfloat16 [512, 16, 384], P('chan', 'seg')
- taper_len: int32 [512], P('chan'), may hold values from 1 to 192
- gather_id: int32 [512, 512], P('chan'), may hold values from 0 to 511, as said below
- offset_bin: int32 [512, 512], P('chan'), may hold values from 0 to 1, as said below
Outputs:
- stack: float32 [512, 2, 256], P(('chan', 'seg'))
Inputs may be any that keep to these rules, and one draw needn't show every extreme that they name: Channels lie on a fiber at integer positions p_0 < p_1 < ... with steps of 2 to 5; gather_id[i, j] = floor((p_i + p_j - 2 p_0) * 512 / (2 (p_last - p_0) + 1)). offset_bin[i, j] = floor(|p_i - p_j| * 2 / (p_last - p_0 + 1)) with the same positions.
All inputs are finite; a program needn't handle non-finite values.
Results may differ from a plain program's by a relative error of at most 0.0039.
Values may be sent and summed in bfloat16 or wider, within the bound.
No kernel may reach another device: no remote copies, remote signals or barrier semaphores. Data moves between devices by JAX's collectives and lax.ppermute only.
A program may use at most 64 MiB of HBM per device.

v0:
```python
import math
import jax
import jax.numpy as jnp
from jax import lax
from jax.sharding import PartitionSpec as P

LAGS = 256
OFFBINS = 2


def normalize(traces, taper_len):
    values = traces.astype(jnp.float32)
    sample_count = values.shape[2]
    power = jnp.mean(values * values, axis=2, keepdims=True)
    times = jnp.arange(sample_count).astype(jnp.float32)
    length = taper_len.astype(jnp.float32)[:, None, None]
    window = jnp.minimum(1.0, jnp.minimum((times + 1.0) / length, (sample_count - times) / length))
    return (window * values * lax.rsqrt(power + 1e-06)).astype(jnp.bfloat16)


def hankel(normed, lag_count):
    chan_count, seg_count, sample_count = normed.shape
    turned = jnp.transpose(normed, (1, 2, 0))
    padded = jnp.pad(turned, ((0, 0), (lag_count // 2, lag_count // 2), (0, 0)))
    slices = [padded[:, lag_count - k : lag_count - k + sample_count, :] for k in range(lag_count)]
    picked = jnp.stack(slices, axis=3)
    return picked.reshape(seg_count * sample_count, chan_count * lag_count)


def shards(traces, taper_len, gather_id, offset_bin):
    chan_count = traces.shape[0]
    chan_devices = lax.axis_size("chan")
    seg_devices = lax.axis_size("seg")
    bucket_count = chan_devices * seg_devices * OFFBINS
    normed = normalize(traces, taper_len)
    kernel = hankel(normed, LAGS)
    first_row = lax.axis_index("chan") * chan_count
    own_rows = first_row + jnp.arange(chan_count, dtype=jnp.int32)[None, :]
    empty = jnp.zeros((bucket_count, LAGS), jnp.float32)
    flat = lax.optimization_barrier(normed.reshape(chan_count, -1))
    piece = lax.all_gather(flat, "chan", axis=0, tiled=True)
    row_count = piece.shape[0]
    product = jnp.dot(piece, kernel, preferred_element_type=jnp.float32)
    product = product.reshape(row_count * chan_count, LAGS)
    labels = jnp.transpose(gather_id * OFFBINS + offset_bin)
    partner = jnp.arange(row_count, dtype=jnp.int32)[:, None]
    labels = jnp.where(partner == own_rows, bucket_count, labels).reshape(-1)
    total = empty.at[labels].add(product, mode="drop")
    scale = 1.0 / math.sqrt(traces.shape[2] * traces.shape[1] * seg_devices)
    stacked = (total * scale).reshape(chan_devices, seg_devices, OFFBINS, LAGS)
    stacked = jnp.transpose(stacked, (1, 0, 2, 3))
    part = lax.psum_scatter(stacked, "seg", scatter_dimension=0, tiled=True)
    part = part.reshape(chan_devices, OFFBINS, LAGS)
    result = lax.psum_scatter(part, "chan", scatter_dimension=0, tiled=True)
    return result


def solution(mesh):
    placed = (P("chan", "seg", None), P("chan"), P("chan", None), P("chan", None))
    return jax.shard_map(
        shards,
        mesh=mesh,
        in_specs=placed,
        out_specs=P(("chan", "seg"), None, None),
        check_vma=False,
    )
```

profile of v0, /device:TPU:8, one launch (start us, length us, event | category | flops | bytes accessed | tf_op | source)
XLA Modules:
  0.0 545.1 jit_solution(4039340912734101357)
XLA Ops:
  6.5 0.9 fusion.5
  7.4 0.7 convert_element_type.24
  8.1 0.8 fusion.264
  8.9 0.8 fusion.265
  10.4 0.1 constant_dynamic-update-slice_fusion.246
  10.4 0.1 constant_dynamic-update-slice_fusion.245
  10.5 0.1 constant_dynamic-update-slice_fusion.244
  10.6 0.1 constant_dynamic-update-slice_fusion.243
  10.7 0.1 constant_dynamic-update-slice_fusion.242
  10.8 0.1 constant_dynamic-update-slice_fusion.241
  10.8 0.1 constant_dynamic-update-slice_fusion.240
  10.9 0.1 constant_dynamic-update-slice_fusion.239
  11.0 0.1 constant_dynamic-update-slice_fusion.238
  11.1 0.1 constant_dynamic-update-slice_fusion.237
  11.2 0.1 constant_dynamic-update-slice_fusion.236
  11.3 0.1 constant_dynamic-update-slice_fusion.235
  20.1 0.1 constant_dynamic-update-slice_fusion.127
  30.5 0.8 copy.264
  31.3 84.6 %all_gather.3 = bf16[512,384]{1,0:T(8,128)(2,1)S(1)} all-gather(bf16[16,384]{1,0:T(8,128)(2,1)S(1)} %fusion.265), channel_id=1, replica_groups=mesh['chan'=32,'seg'=16] {'chan'}, dimensions={0}, use_global_device_ids=true | all-gather | bytes 405504 | tf_op jit(solution)/shard_map/all_gather | solution.py:41
  115.9 5.6 %fusion.261 = f32[512,4096]{1,0:T(8,128)} fusion(bf16[512,384]{1,0:T(8,128)(2,1)S(1)} %all_gather.3, bf16[384,4096]{0,1:T(8,128)(2,1)S(1)} %bitcast.1036), kind=kOutput, calls=%fused_computation.785 | convolution fusion | flops 1610612736 | bytes 11927552 | tf_op jit(solution)/shard_map/dot_general | solution.py:43
  121.5 9.3 %reshape.176 = f32[8192,256]{1,0:T(8,128)} reshape(f32[512,4096]{1,0:T(8,128)} %fusion.261) | data formatting | bytes 16777216 | tf_op jit(solution)/shard_map/reshape | solution.py:44
  130.9 0.1 copy.263
  131.0 0.2 reshape.166
  131.2 44.9 %scatter_custom_fusion = f32[1024,256]{1,0:T(8,128)S(1)} fusion(s32[8192]{0:T(1024)S(1)} %bitcast.1039, f32[8192,256]{1,0:T(8,128)} %reshape.176, f32[]{:T(128)} %constant.13.clone.1), kind=kCustom, calls=%fused_computation.258 | custom fusion | flops 2097152 | bytes 1049088 | tf_op jit(solution)/shard_map/scatter-add | solution.py:48
  176.1 0.1 broadcast_multiply_fusion
  176.2 0.6 reshape.170
  176.8 1.6 copy.265
  178.5 56.0 %reduce-scatter.2.cloned.1.call-done = f32[1,32,2,256]{3,1,2,0:T(8,128)} async-done(((f32[16,32,2,256]{3,1,2,0:T(8,128)}), f32[1,32,2,256]{3,1,2,0:T(8,128)}) %reduce-scatter.2.cloned.1.call-update) | async-done | bytes 65552 | tf_op jit(solution)/shard_map/reduce_scatter | solution.py:52
  234.5 1.5 copy.266
  236.0 1.3 dynamic-slice
  237.3 299.2 %all-reduce.4.cloned.1.call-done = f32[32,2,256]{2,1,0:T(2,128)} async-done(((f32[32,2,256]{2,1,0:T(2,128)}), f32[32,2,256]{2,1,0:T(2,128)}) %all-reduce.4.cloned.1.call-update) | async-done | bytes 65552
  536.5 1.8 constant_dynamic-slice_fusion
  (258 shorter events, 19.8 us)
Async XLA Ops:
  6.5 13.5 %copy-start = (bf16[16,1,384]{2,0,1:T(8,128)(2,1)S(1)}, bf16[16,1,384]{2,0,1:T(8,128)(2,1)}, u32[]{:S(2)}) copy-start(bf16[16,1,384]{2,0,1:T(8,128)(2,1)} %param.4) | copy-start | bytes 36868
  6.5 227.9 %reduce-scatter.2.cloned.1.call-start = ((), (), s32[]{:S(2)}) async-start(), calls=%async_computation.1 | async-start | bytes 1114112 | tf_op jit(solution)/shard_map/reduce_scatter | solution.py:52
  121.5 9.3 %copy-start.1 = (s32[16,512]{1,0:T(8,128)S(1)}, s32[16,512]{1,0:T(8,128)}, u32[]{:S(2)}) copy-start(s32[16,512]{1,0:T(8,128)} %param.7) | copy-start | bytes 98308
  121.5 9.3 %copy-start.2 = (s32[16,512]{1,0:T(8,128)S(1)}, s32[16,512]{1,0:T(8,128)}, u32[]{:S(2)}) copy-start(s32[16,512]{1,0:T(8,128)} %param.6) | copy-start | bytes 98308
  178.4 358.1 %all-reduce.4.cloned.1.call-start = ((), (), s32[]{:S(2)}) async-start(), calls=%async_computation.2 | async-start | bytes 131072
Sparse Core Ops, SparseCore 0:
  178.6 55.8 reduce-scatter.1
  237.6 298.8 all-reduce.3
where the time goes:
time: 546 us; the launch traced here: 545 us
  waiting for transfers between devices  355 us (65%)
  blocking collectives  84.6 us (15%)
  other arithmetic  48.3 us (9%)
  local copies, waits for them, and re-layouts  37.7 us (7%)
  between operations  13.6 us (2%)
  matrix products  5.6 us (1%)
    unnamed x3, waiting for transfers between devices  299 us
    all_gather x1, blocking collectives, shards(): piece = lax.all_gather(flat, 'chan', axis=0, tiled=True)  84.6 us
    reduce_scatter x1, waiting for transfers between devices, shards(): part = lax.psum_scatter(stacked, 'seg', scatter_dimension=0, tiled=True)  56 us
    scatter-add x1, other arithmetic, shards(): total = empty.at[labels].add(product, mode='drop')  44.9 us
    unnamed x262, local copies, waits for them, and re-layouts  23.6 us
  transfers between devices with their start and end apart: 2, of which 2 were waited for; matrix products, arithmetic and copies ran while one was open for 0% of the time, Pallas kernels for 0%

commit v1 on v0

--- a/solution.py
+++ b/solution.py
@@ -38,7 +38,9 @@
     own_rows = first_row + jnp.arange(chan_count, dtype=jnp.int32)[None, :]
     empty = jnp.zeros((bucket_count, LAGS), jnp.float32)
     flat = lax.optimization_barrier(normed.reshape(chan_count, -1))
-    piece = lax.all_gather(flat, "chan", axis=0, tiled=True)
+    piece = jnp.concatenate(
+        lax.all_to_all(jnp.stack([flat] * lax.axis_size("chan")), "chan", 0, 0), axis=0
+    )
     row_count = piece.shape[0]
     product = jnp.dot(piece, kernel, preferred_element_type=jnp.float32)
     product = product.reshape(row_count * chan_count, LAGS)

time: 546 us -> 493 us (0.903)
  blocking collectives: 84.6 us -> 0 us
  starting transfers between devices: 0.04 us -> 18 us
  waiting for transfers between devices: 355 us -> 363 us
    all_gather x1 -> x0, blocking collectives: 84.6 us -> none  [shards(): piece = lax.all_gather(flat, 'chan', axis=0, tiled=True)]
    all_to_all x0 -> x1, starting transfers between devices: none -> 17.9 us  [shards(): lax.all_to_all(jnp.stack([flat] * lax.axis_size('chan')), 'chan', 0, 0)]
    reduce_scatter x1, waiting for transfers between devices: 56 us -> 63.5 us  [shards(): part = lax.psum_scatter(stacked, 'seg', scatter_dimension=0, tiled=True)]
    unnamed x262 -> x258, local copies, waits for them, and re-layouts: 23.6 us -> 23.6 us
  transfers between devices with their start and end apart: 2 -> 3, of which waited for: 2 -> 2; matrix products, arithmetic and copies ran while one was open for 0% -> 6% of each run, Pallas kernels for 0% -> 0%
where the time goes in v1:
time: 493 us; the launch traced here: 492 us
  waiting for transfers between devices  363 us (74%)
  other arithmetic  51 us (10%)
  local copies, waits for them, and re-layouts  41.5 us (8%)
  starting transfers between devices  18 us (4%)
  between operations  13.6 us (3%)
  matrix products  5.58 us (1%)
    unnamed x3, waiting for transfers between devices  299 us
    reduce_scatter x1, waiting for transfers between devices, shards(): part = lax.psum_scatter(stacked, 'seg', scatter_dimension=0, tiled=True)  63.5 us
    scatter-add x1, other arithmetic, shards(): total = empty.at[labels].add(product, mode='drop')  44.9 us
    unnamed x258, local copies, waits for them, and re-layouts  23.6 us
    all_to_all x1, starting transfers between devices, shards(): lax.all_to_all(jnp.stack([flat] * lax.axis_size('chan')), 'chan', 0, 0)  17.9 us
  transfers between devices with their start and end apart: 3, of which 2 were waited for; matrix products, arithmetic and copies ran while one was open for 6% of the time, Pallas kernels for 0%

profile of v1, /device:TPU:8, one launch (start us, length us, event | category | flops | bytes accessed | tf_op | source)
XLA Modules:
  0.0 492.3 jit_solution(4138335215433166690)
XLA Ops:
  6.5 0.9 fusion.5
  7.4 0.7 convert_element_type.24
  8.1 0.8 fusion.265
  8.9 0.8 stack.806
  9.7 17.9 %all-to-all-start = ((bf16[32,16,384]{2,1,0:T(8,128)(2,1)}), bf16[32,16,384]{2,1,0:T(8,128)(2,1)S(1)}, u32[]{:S(2)}, u32[]{:S(2)}) async-start(bf16[32,16,384]{2,1,0:T(8,128)(2,1)} %stack.806), calls=%async_computation | async-start | bytes 786432 | tf_op jit(solution)/shard_map/all_to_all | solution.py:42
  27.7 0.8 fusion.264
  29.0 0.1 constant_dynamic-update-slice_fusion.248
  29.0 0.1 constant_dynamic-update-slice_fusion.247
  29.1 0.1 constant_dynamic-update-slice_fusion.246
  29.2 0.1 constant_dynamic-update-slice_fusion.245
  29.3 0.1 constant_dynamic-update-slice_fusion.244
  29.4 0.1 constant_dynamic-update-slice_fusion.243
  29.4 0.1 constant_dynamic-update-slice_fusion.242
  29.5 0.1 constant_dynamic-update-slice_fusion.241
  30.2 0.1 constant_dynamic-update-slice_fusion.233
  38.8 0.1 constant_dynamic-update-slice_fusion.127
  49.3 0.8 copy.264
  50.1 1.4 bitcast_select_fusion
  51.5 1.6 copy.263
  53.1 1.7 reshape.171
  54.8 1.4 compare_select_fusion
  56.2 5.6 %fusion.261 = f32[512,4096]{1,0:T(8,128)} fusion(bf16[512,384]{1,0:T(8,128)(2,1)S(1)} %bitcast.1039, bf16[384,4096]{0,1:T(8,128)(2,1)S(1)} %bitcast.1037), kind=kOutput, calls=%fused_computation.785 | convolution fusion | flops 1610612736 | bytes 11927552 | tf_op jit(solution)/shard_map/dot_general | solution.py:45
  61.8 9.3 %reshape.182 = f32[8192,256]{1,0:T(8,128)} reshape(f32[512,4096]{1,0:T(8,128)} %fusion.261) | data formatting | bytes 16777216 | tf_op jit(solution)/shard_map/reshape | solution.py:46
  71.1 44.9 %scatter_custom_fusion = f32[1024,256]{1,0:T(8,128)S(1)} fusion(s32[8192]{0:T(1024)} %bitcast.1041, f32[8192,256]{1,0:T(8,128)} %reshape.182, f32[]{:T(128)} %constant.13.clone.1), kind=kCustom, calls=%fused_computation.258 | custom fusion | flops 2097152 | bytes 1049088 | tf_op jit(solution)/shard_map/scatter-add | solution.py:50
  115.9 0.1 broadcast_multiply_fusion
  116.0 0.6 reshape.176
  116.7 1.6 copy.265
  118.3 63.5 %reduce-scatter.2.cloned.1.call-done = f32[1,32,2,256]{3,1,2,0:T(8,128)} async-done(((f32[16,32,2,256]{3,1,2,0:T(8,128)}), f32[1,32,2,256]{3,1,2,0:T(8,128)}) %reduce-scatter.2.cloned.1.call-update) | async-done | bytes 65552 | tf_op jit(solution)/shard_map/reduce_scatter | solution.py:54
  181.9 1.5 copy.266
  183.4 1.3 dynamic-slice
  184.7 299.0 %all-reduce.4.cloned.1.call-done = f32[32,2,256]{2,1,0:T(2,128)} async-done(((f32[32,2,256]{2,1,0:T(2,128)}), f32[32,2,256]{2,1,0:T(2,128)}) %all-reduce.4.cloned.1.call-update) | async-done | bytes 65552
  483.7 1.8 constant_dynamic-slice_fusion
  (256 shorter events, 20.0 us)
Async XLA Ops:
  6.5 32.3 %copy-start = (bf16[16,1,384]{2,0,1:T(8,128)(2,1)S(1)}, bf16[16,1,384]{2,0,1:T(8,128)(2,1)}, u32[]{:S(2)}) copy-start(bf16[16,1,384]{2,0,1:T(8,128)(2,1)} %param.4) | copy-start | bytes 36868
  9.7 46.5 %all-to-all-start = ((bf16[32,16,384]{2,1,0:T(8,128)(2,1)}), bf16[32,16,384]{2,1,0:T(8,128)(2,1)S(1)}, u32[]{:S(2)}, u32[]{:S(2)}) async-start(bf16[32,16,384]{2,1,0:T(8,128)(2,1)} %stack.806), calls=%async_computation | async-start | bytes 786432 | tf_op jit(solution)/shard_map/all_to_all | solution.py:42
  27.6 154.2 %reduce-scatter.2.cloned.1.call-start = ((), (), s32[]{:S(2)}) async-start(), calls=%async_computation.2 | async-start | bytes 1114112 | tf_op jit(solution)/shard_map/reduce_scatter | solution.py:54
  118.3 365.4 %all-reduce.4.cloned.1.call-start = ((), (), s32[]{:S(2)}) async-start(), calls=%async_computation.3 | async-start | bytes 131072
Sparse Core Ops, SparseCore 0:
  118.4 63.4 reduce-scatter.1
  185.0 298.6 all-reduce.3
